TPU v7x, 512 devices: a whole 4x8x8 slice. The times are simulated.
512 devices in a mesh: tiles: 128 (over z, y, core), rep: 4 (over x).
Axes of the slice: x: 4, y: 8, z: 8, core: 2. Of those that a mesh axis runs over, the one named last changes fastest.
Arguments:
- tile_data: float32 [1536, 64, 4096], P(('tiles', 'rep')), may hold values from -64 to 64
- tile_coords: int32 [1536, 3], P(('tiles', 'rep')), may hold values from 0 to 127, as said below
- tile_count: int32 [512], P(('tiles', 'rep')), may hold values from 1 to 3, 1024 in all
- weights: int32 [1536], P(('tiles', 'rep')), may hold values from 1 to 4
- owner_map: int32 [128], replicated, may hold values from 0 to 127, as said below
- factor_b: bfloat16 [8192, 256], P(('tiles', 'rep'))
- factor_c: bfloat16 [1024, 256], replicated
Outputs:
- updated: float32 [8192, 256], P(('tiles', 'rep'))
Inputs may be any that keep to these rules, and one draw needn't show every extreme that they name: `tile_coords`: columns 0 and 1 name row blocks below 128, column 2 a block below 16. Every slot of device d = t * 4 + e has owner_map[i_s] = t. Among the 3 slots of one device the positions owner_map[j_s] all differ. `owner_map`: A permutation of the 128 row blocks.
All inputs are finite; a program needn't handle non-finite values. No bound on the sum of `tile_count` on one device may be relied on, other than what follows from the above.
Results may differ from a plain program's by a relative error of at most 0.0095.
Values may be sent and summed in bfloat16 or wider, within the bound.
No kernel may reach another device: no remote copies, remote signals or barrier semaphores. Data moves between devices by JAX's collectives and lax.ppermute only.
A program may use at most 128 MiB of HBM per device.

v0:
```python
import jax
import jax.numpy as jnp
from jax import lax
from jax.sharding import PartitionSpec as P


def per_device(tile_data, tile_coords, tile_count, weights, owner_map, factor_b, factor_c):
    slot_total = tile_data.shape[0]
    tile_edge = tile_data.shape[1]
    rank_cols = factor_b.shape[1]
    is_live = jnp.arange(slot_total, dtype=jnp.int32) < tile_count[0]
    slot_scale = weights.astype(jnp.float32) * is_live.astype(jnp.float32)
    stored_second = jnp.take(owner_map, tile_coords[:, 1])
    block_offsets = jnp.arange(tile_edge, dtype=jnp.int32)
    initial = jnp.zeros((slot_total, tile_edge, rank_cols), jnp.bfloat16)
    owned = lax.all_gather(factor_b, "rep", axis=0, tiled=True)
    row_piece = lax.all_gather(owned, "tiles", axis=0, tiled=True)
    piece_rows = row_piece.shape[0]
    wanted = stored_second[:, None] * tile_edge + block_offsets[None, :]
    inside = (wanted >= 0) & (wanted < piece_rows)
    taken = jnp.take(row_piece, jnp.clip(wanted, 0, piece_rows - 1), axis=0)
    blocks = jnp.where(inside[:, :, None], taken, initial)
    summed = jnp.zeros((tile_edge, rank_cols), jnp.float32)
    for position in range(slot_total):
        c_block = lax.dynamic_slice_in_dim(
            factor_c, tile_coords[position, 2] * tile_edge, tile_edge, 0
        ).astype(jnp.float32)
        flat_tile = tile_data[position].reshape(tile_edge * tile_edge, tile_edge)
        inner_sum = jnp.dot(flat_tile, c_block, precision=lax.Precision.HIGHEST)
        inner_sum = inner_sum.reshape(tile_edge, tile_edge, rank_cols)
        partial_value = jnp.einsum("ijr,jr->ir", inner_sum, blocks[position].astype(jnp.float32))
        rounded = (partial_value * slot_scale[position]).astype(jnp.bfloat16)
        summed = summed + rounded.astype(jnp.float32)
    my_rows = lax.psum_scatter(summed, "rep", scatter_dimension=0, tiled=True)
    own_gram = jnp.dot(factor_b.T, factor_b, preferred_element_type=jnp.float32)
    gram_b = lax.psum(own_gram, ("tiles", "rep"))
    gram_c = jnp.dot(factor_c.T, factor_c, preferred_element_type=jnp.float32)
    normal_matrix = gram_b * gram_c
    lower_factor = jnp.linalg.cholesky(normal_matrix)
    return jax.scipy.linalg.cho_solve((lower_factor, True), my_rows.T).T


def solution(mesh):
    in_specs = (
        P(("tiles", "rep"), None, None),
        P(("tiles", "rep"), None),
        P(("tiles", "rep")),
        P(("tiles", "rep")),
        P(),
        P(("tiles", "rep"), None),
        P(),
    )
    out_specs = P(("tiles", "rep"), None)
    return jax.shard_map(
        per_device, mesh=mesh, in_specs=in_specs, out_specs=out_specs, check_vma=False
    )
```

profile of v0, /device:TPU:23, one launch (start us, length us, event | category | flops | bytes accessed | tf_op | source)
XLA Modules:
  0.0 374.4 jit_solution(15148988416922388078)
XLA Ops:
  7.4 1.7 fusion.28
  9.1 10.0 %all_gather.6 = bf16[64,256]{1,0:T(8,128)(2,1)} all-gather(bf16[16,256]{1,0:T(8,128)(2,1)} %param.12), channel_id=1, replica_groups=mesh['tiles'=128,'rep'=4] {'rep'}, dimensions={0}, use_global_device_ids=true | all-gather | bytes 40960 | tf_op jit(solution)/shard_map/all_gather | solution.py:16
  19.2 0.8 slice.101
  19.9 1.5 fusion.26
  23.5 1.3 gather_fusion
  25.0 3.7 fusion.25
  28.7 2.0 reshape_squeeze.9
  30.7 3.9 %convolution_bitcast_fusion.2 = f32[4096,256]{0,1:T(8,128)} fusion(f32[4096,64]{1,0:T(8,128)S(1)} %reshape_squeeze.9, bf16[1024,256]{1,0:T(8,128)(2,1)S(1)} %copy-done, s32[]{:T(128)S(6)} %select_n.56), kind=kOutput, calls=%fused_computation.6 | convolution fusion | flops 805306368 | bytes 6324228 | tf_op jit(solution)/shard_map/dot_general | solution.py:29
  34.7 5.6 %copy.50 = f32[4096,256]{1,0:T(8,128)} copy(f32[4096,256]{0,1:T(8,128)} %convolution_bitcast_fusion.2) | data formatting | bytes 8388608
  40.3 2.0 reshape_squeeze.11
  42.3 3.9 %convolution_bitcast_fusion = f32[4096,256]{0,1:T(8,128)} fusion(f32[4096,64]{1,0:T(8,128)S(1)} %reshape_squeeze.11, bf16[1024,256]{1,0:T(8,128)(2,1)S(1)} %copy-done, s32[]{:T(128)S(6)} %select_n.58), kind=kOutput, calls=%fused_computation.4 | convolution fusion | flops 805306368 | bytes 6324228 | tf_op jit(solution)/shard_map/dot_general | solution.py:29
  46.2 5.6 %copy.52 = f32[4096,256]{1,0:T(8,128)} copy(f32[4096,256]{0,1:T(8,128)} %convolution_bitcast_fusion) | data formatting | bytes 8388608
  51.8 2.0 reshape_squeeze.10
  53.8 3.9 %convolution_bitcast_fusion.1 = f32[4096,256]{0,1:T(8,128)} fusion(f32[4096,64]{1,0:T(8,128)S(1)} %reshape_squeeze.10, bf16[1024,256]{1,0:T(8,128)(2,1)S(1)} %copy-done, s32[]{:T(128)S(6)} %select_n.57), kind=kOutput, calls=%fused_computation.5 | convolution fusion | flops 805306368 | bytes 6324228 | tf_op jit(solution)/shard_map/dot_general | solution.py:29
  57.7 5.7 %copy.51 = f32[4096,256]{1,0:T(8,128)} copy(f32[4096,256]{0,1:T(8,128)} %convolution_bitcast_fusion.1) | data formatting | bytes 8388608
  64.8 223.5 %all-reduce.3.cloned.1.call-done = f32[256,256]{0,1:T(8,128)} async-done(((f32[256,256]{0,1:T(8,128)}), f32[256,256]{0,1:T(8,128)}) %all-reduce.3.cloned.1.call-update) | async-done | bytes 262160 | tf_op jit(solution)/shard_map/psum | solution.py:36
  288.3 1.3 convolution_multiply_fusion
  289.8 11.7 %cholesky.50 = f32[128,128]{1,0:T(8,128)S(1)} custom-call(f32[128,128]{1,0:T(8,128)S(1)} %cholesky.118), custom_call_target="Cholesky" | custom-call | tf_op jit(solution)/shard_map/jit(cholesky)/cholesky | solution.py:39
  301.5 9.8 %custom-call.18 = f32[1,128,128]{1,2,0:T(8,128)S(1)} custom-call(f32[1,128,128]{2,1,0:T(8,128)S(1)} %get-tuple-element.32), custom_call_target="InvertDiagBlocksLowerTriangular" | custom-call | tf_op jit(solution)/shard_map/jit(cholesky)/cholesky | solution.py:39
  311.8 11.7 %cholesky.105 = f32[128,128]{1,0:T(8,128)S(1)} custom-call(f32[128,128]{1,0:T(8,128)S(1)} %convolution_subtract_fusion), custom_call_target="Cholesky" | custom-call | tf_op jit(solution)/shard_map/jit(cholesky)/cholesky | solution.py:39
  323.6 0.7 compare_reduce_fusion
  325.6 3.6 gather_fusion.1
  329.3 3.0 multiply_reduce_fusion.2
  332.5 4.9 %multiply_reduce_fusion = (f32[256,64]{0,1:T(8,128)S(1)}, f32[256,64]{0,1:T(8,128)S(1)}) fusion(f32[256,64]{0,1:T(8,128)S(1)} %get-tuple-element.26, f32[4096,256]{1,0:T(8,128)} %copy.52, f32[4096,256]{1,0:T(8,128)} %copy.51, f32[256,64]{0,1:T(8,128)S(1)} %get-tuple-element.27), kind=kLoop, calls=%fused_computation.7 | loop fusion | flops 4161536 | bytes 8650752
  337.6 1.9 add_bitcast_fusion
  339.5 0.7 copy.53
  340.3 3.8 %while.1 = (s32[]{:T(128)}, f32[256,256]{1,0:T(8,128)S(1)}, s32[2,2]{1,0:T(2,128)S(1)}, f32[2,128,128]{2,1,0:T(8,128)S(1)}, s32[]{:T(128)}) while((s32[]{:T(128)}, f32[256,256]{1,0:T(8,128)S(1)}, s32[2,2]{1,0:T(2,128)S(1)}, f32[2,128,128]{2,1,0:T(8,128)S(1)}, s32[]{:T(128)}) %tuple.33), condition=%wide.while_cond, body=%wide.while_body.sunk | while | flops 2 | bytes 131189 | solution.py:40
  340.9 1.3 bitcast_dynamic-update-slice_fusion.2
  342.8 1.3 bitcast_dynamic-update-slice_fusion.2
  344.1 19.7 %custom-call.19 = f32[2,128,128]{1,2,0:T(8,128)S(1)} custom-call(f32[2,128,128]{2,1,0:T(8,128)S(1)} %get-tuple-element.12), custom_call_target="InvertDiagBlocksLowerTriangular" | custom-call | tf_op jit(solution)/shard_map/jit(_cho_solve)/triangular_solve | solution.py:40
  363.8 0.9 fusion.5
  364.7 0.9 convolution_subtract_fusion.2
  (48 shorter events, 5.1 us)
Async XLA Ops:
  7.4 23.4 %copy-start = (bf16[1024,256]{1,0:T(8,128)(2,1)S(1)}, bf16[1024,256]{1,0:T(8,128)(2,1)}, u32[]{:S(2)}) copy-start(bf16[1024,256]{1,0:T(8,128)(2,1)} %param.13) | copy-start | bytes 1572868
  7.4 280.9 %all-reduce.3.cloned.1.call-start = ((), (), s32[]{:S(2)}) async-start(), calls=%async_computation.1 | async-start | bytes 524288 | tf_op jit(solution)/shard_map/psum | solution.py:36
  9.1 316.5 %all-gather.2.cloned.1.call-start = ((), (), s32[]{:S(2)}) async-start(), calls=%async_computation.2 | async-start | bytes 4227072 | tf_op jit(solution)/shard_map/all_gather | solution.py:17
  19.1 344.7 %reduce-scatter.4.cloned.1.call-start = ((), (), s32[]{:S(2)}) async-start(), calls=%async_computation.3 | async-start | bytes 81920 | tf_op jit(solution)/shard_map/reduce_scatter | solution.py:34
  57.7 6.3 %copy-start.1 = (s32[3]{0:T(128)S(1)}, s32[3]{0:T(128)}, u32[]{:S(2)}) copy-start(s32[3]{0:T(128)} %param.10) | copy-start | bytes 40
Sparse Core Ops, SparseCore 0:
  13.2 275.0 all-reduce.2
Sparse Core Ops, SparseCore 1:
  19.2 92.1 all-gather.1
  340.3 17.2 reduce-scatter.3
where the time goes:
time: 375 us; the launch traced here: 374 us
  waiting for transfers between devices  224 us (60%)
  other arithmetic  64.6 us (17%)
  local copies, waits for them, and re-layouts  39.5 us (11%)
  between operations  19 us (5%)
  matrix products  17.7 us (5%)
  blocking collectives  9.96 us (3%)
    psum x1, waiting for transfers between devices, per_device(): gram_b = lax.psum(own_gram, ('tiles', 'rep'))  223 us
    another operation x6, other arithmetic, per_device(): lower_factor = jnp.linalg.cholesky(normal_matrix)  34 us
    another operation x3, other arithmetic, per_device(): return jax.scipy.linalg.cho_solve((lower_factor, True), my_rows.T).T  19.7 us
    unnamed x9, local copies, waits for them, and re-layouts  17.7 us
    dot_general x3, matrix products, per_device(): inner_sum = jnp.dot(flat_tile, c_block, precision=lax.Precision.HIGHEST)  11.7 us
    all_gather x1, blocking collectives, per_device(): owned = lax.all_gather(factor_b, 'rep', axis=0, tiled=True)  9.96 us
    unnamed x4, other arithmetic  7.99 us
  transfers between devices with their start and end apart: 3, of which 1 were waited for; matrix products, arithmetic and copies ran while one was open for 27% of the time, Pallas kernels for 0%

commit v1 on v0

--- a/solution.py
+++ b/solution.py
@@ -13,7 +13,9 @@
     stored_second = jnp.take(owner_map, tile_coords[:, 1])
     block_offsets = jnp.arange(tile_edge, dtype=jnp.int32)
     initial = jnp.zeros((slot_total, tile_edge, rank_cols), jnp.bfloat16)
-    owned = lax.all_gather(factor_b, "rep", axis=0, tiled=True)
+    owned = jnp.concatenate(
+        lax.all_to_all(jnp.stack([factor_b] * lax.axis_size("rep")), "rep", 0, 0), axis=0
+    )
     row_piece = lax.all_gather(owned, "tiles", axis=0, tiled=True)
     piece_rows = row_piece.shape[0]
     wanted = stored_second[:, None] * tile_edge + block_offsets[None, :]

time: 375 us -> 375 us (level)
    all_gather x1 -> x0, blocking collectives: 9.96 us -> none  [per_device(): owned = lax.all_gather(factor_b, 'rep', axis=0, tiled=True)]
    all_to_all x0 -> x1, blocking collectives: none -> 6.62 us  [per_device(): lax.all_to_all(jnp.stack([factor_b] * lax.axis_size('rep')), 'rep', 0, 0)]
  transfers between devices with their start and end apart: 3 -> 3, of which waited for: 1 -> 1; matrix products, arithmetic and copies ran while one was open for 27% -> 28% of each run, Pallas kernels for 0% -> 0%
where the time goes in v1:
time: 375 us; the launch traced here: 374 us
  waiting for transfers between devices  226 us (60%)
  other arithmetic  64.6 us (17%)
  local copies, waits for them, and re-layouts  40.2 us (11%)
  between operations  19 us (5%)
  matrix products  17.7 us (5%)
  blocking collectives  6.62 us (2%)
    psum x1, waiting for transfers between devices, per_device(): gram_b = lax.psum(own_gram, ('tiles', 'rep'))  226 us
    another operation x6, other arithmetic, per_device(): lower_factor = jnp.linalg.cholesky(normal_matrix)  34 us
    another operation x3, other arithmetic, per_device(): return jax.scipy.linalg.cho_solve((lower_factor, True), my_rows.T).T  19.7 us
    unnamed x9, local copies, waits for them, and re-layouts  17.7 us
    dot_general x3, matrix products, per_device(): inner_sum = jnp.dot(flat_tile, c_block, precision=lax.Precision.HIGHEST)  11.7 us
    unnamed x4, other arithmetic  7.99 us
  transfers between devices with their start and end apart: 3, of which 1 were waited for; matrix products, arithmetic and copies ran while one was open for 28% of the time, Pallas kernels for 0%

profile of v1, /device:TPU:23, one launch (start us, length us, event | category | flops | bytes accessed | tf_op | source)
XLA Modules:
  0.0 374.1 jit_solution(5239192876259579610)
XLA Ops:
  7.4 1.7 fusion.28
  9.1 0.7 stack.2
  9.8 6.6 %all_to_all.5 = bf16[4,16,256]{2,1,0:T(8,128)(2,1)} all-to-all(bf16[4,16,256]{2,1,0:T(8,128)(2,1)S(1)} %stack.2), channel_id=1, replica_groups=mesh['tiles'=128,'rep'=4] {'rep'}, dimensions={0} | all-to-all | bytes 65536 | tf_op jit(solution)/shard_map/all_to_all | solution.py:17
  16.6 0.8 slice.101
  17.3 1.5 fusion.26
  20.9 1.3 gather_fusion
  22.4 3.7 fusion.25
  26.1 2.0 reshape_squeeze.9
  28.1 3.9 %convolution_bitcast_fusion.2 = f32[4096,256]{0,1:T(8,128)} fusion(f32[4096,64]{1,0:T(8,128)S(1)} %reshape_squeeze.9, bf16[1024,256]{1,0:T(8,128)(2,1)S(1)} %copy-done, s32[]{:T(128)S(6)} %select_n.56), kind=kOutput, calls=%fused_computation.6 | convolution fusion | flops 805306368 | bytes 6324228 | tf_op jit(solution)/shard_map/dot_general | solution.py:31
  32.0 5.6 %copy.50 = f32[4096,256]{1,0:T(8,128)} copy(f32[4096,256]{0,1:T(8,128)} %convolution_bitcast_fusion.2) | data formatting | bytes 8388608
  37.6 2.0 reshape_squeeze.11
  39.7 3.9 %convolution_bitcast_fusion = f32[4096,256]{0,1:T(8,128)} fusion(f32[4096,64]{1,0:T(8,128)S(1)} %reshape_squeeze.11, bf16[1024,256]{1,0:T(8,128)(2,1)S(1)} %copy-done, s32[]{:T(128)S(6)} %select_n.58), kind=kOutput, calls=%fused_computation.4 | convolution fusion | flops 805306368 | bytes 6324228 | tf_op jit(solution)/shard_map/dot_general | solution.py:31
  43.6 5.6 %copy.52 = f32[4096,256]{1,0:T(8,128)} copy(f32[4096,256]{0,1:T(8,128)} %convolution_bitcast_fusion) | data formatting | bytes 8388608
  49.2 2.0 reshape_squeeze.10
  51.2 3.9 %convolution_bitcast_fusion.1 = f32[4096,256]{0,1:T(8,128)} fusion(f32[4096,64]{1,0:T(8,128)S(1)} %reshape_squeeze.10, bf16[1024,256]{1,0:T(8,128)(2,1)S(1)} %copy-done, s32[]{:T(128)S(6)} %select_n.57), kind=kOutput, calls=%fused_computation.5 | convolution fusion | flops 805306368 | bytes 6324228 | tf_op jit(solution)/shard_map/dot_general | solution.py:31
  55.1 5.7 %copy.51 = f32[4096,256]{1,0:T(8,128)} copy(f32[4096,256]{0,1:T(8,128)} %convolution_bitcast_fusion.1) | data formatting | bytes 8388608
  62.2 225.8 %all-reduce.3.cloned.1.call-done = f32[256,256]{0,1:T(8,128)} async-done(((f32[256,256]{0,1:T(8,128)}), f32[256,256]{0,1:T(8,128)}) %all-reduce.3.cloned.1.call-update) | async-done | bytes 262160 | tf_op jit(solution)/shard_map/psum | solution.py:38
  288.0 1.3 convolution_multiply_fusion
  289.5 11.7 %cholesky.50 = f32[128,128]{1,0:T(8,128)S(1)} custom-call(f32[128,128]{1,0:T(8,128)S(1)} %cholesky.118), custom_call_target="Cholesky" | custom-call | tf_op jit(solution)/shard_map/jit(cholesky)/cholesky | solution.py:41
  301.2 9.8 %custom-call.18 = f32[1,128,128]{1,2,0:T(8,128)S(1)} custom-call(f32[1,128,128]{2,1,0:T(8,128)S(1)} %get-tuple-element.32), custom_call_target="InvertDiagBlocksLowerTriangular" | custom-call | tf_op jit(solution)/shard_map/jit(cholesky)/cholesky | solution.py:41
  311.5 11.7 %cholesky.105 = f32[128,128]{1,0:T(8,128)S(1)} custom-call(f32[128,128]{1,0:T(8,128)S(1)} %convolution_subtract_fusion), custom_call_target="Cholesky" | custom-call | tf_op jit(solution)/shard_map/jit(cholesky)/cholesky | solution.py:41
  325.3 3.6 gather_fusion.1
  329.0 3.0 multiply_reduce_fusion.2
  332.2 4.9 %multiply_reduce_fusion = (f32[256,64]{0,1:T(8,128)S(1)}, f32[256,64]{0,1:T(8,128)S(1)}) fusion(f32[256,64]{0,1:T(8,128)S(1)} %get-tuple-element.26, f32[4096,256]{1,0:T(8,128)} %copy.52, f32[4096,256]{1,0:T(8,128)} %copy.51, f32[256,64]{0,1:T(8,128)S(1)} %get-tuple-element.27), kind=kLoop, calls=%fused_computation.7 | loop fusion | flops 4161536 | bytes 8650752
  337.3 1.9 add_bitcast_fusion
  339.2 0.7 copy.53
  340.0 3.8 %while.1 = (s32[]{:T(128)}, f32[256,256]{1,0:T(8,128)S(1)}, s32[2,2]{1,0:T(2,128)S(1)}, f32[2,128,128]{2,1,0:T(8,128)S(1)}, s32[]{:T(128)}) while((s32[]{:T(128)}, f32[256,256]{1,0:T(8,128)S(1)}, s32[2,2]{1,0:T(2,128)S(1)}, f32[2,128,128]{2,1,0:T(8,128)S(1)}, s32[]{:T(128)}) %tuple.33), condition=%wide.while_cond, body=%wide.while_body.sunk | while | flops 2 | bytes 131189 | solution.py:42
  340.6 1.3 bitcast_dynamic-update-slice_fusion.2
  342.5 1.3 bitcast_dynamic-update-slice_fusion.2
  343.8 19.7 %custom-call.19 = f32[2,128,128]{1,2,0:T(8,128)S(1)} custom-call(f32[2,128,128]{2,1,0:T(8,128)S(1)} %get-tuple-element.12), custom_call_target="InvertDiagBlocksLowerTriangular" | custom-call | tf_op jit(solution)/shard_map/jit(_cho_solve)/triangular_solve | solution.py:42
  363.5 0.9 fusion.5
  364.4 0.9 convolution_subtract_fusion.2
  (49 shorter events, 5.8 us)
Async XLA Ops:
  7.4 20.7 %copy-start = (bf16[1024,256]{1,0:T(8,128)(2,1)S(1)}, bf16[1024,256]{1,0:T(8,128)(2,1)}, u32[]{:S(2)}) copy-start(bf16[1024,256]{1,0:T(8,128)(2,1)} %param.13) | copy-start | bytes 1572868
  7.4 280.6 %all-reduce.3.cloned.1.call-start = ((), (), s32[]{:S(2)}) async-start(), calls=%async_computation.2 | async-start | bytes 524288 | tf_op jit(solution)/shard_map/psum | solution.py:38
  9.1 316.2 %all-gather.2.cloned.1.call-start = ((), (), s32[]{:S(2)}) async-start(), calls=%async_computation.3 | async-start | bytes 4227072 | tf_op jit(solution)/shard_map/all_gather | solution.py:19
  16.5 347.0 %reduce-scatter.4.cloned.1.call-start = ((), (), s32[]{:S(2)}) async-start(), calls=%async_computation.4 | async-start | bytes 81920 | tf_op jit(solution)/shard_map/reduce_scatter | solution.py:36
  55.1 6.3 %copy-start.1 = (s32[3]{0:T(128)S(1)}, s32[3]{0:T(128)}, u32[]{:S(2)}) copy-start(s32[3]{0:T(128)} %param.10) | copy-start | bytes 40
Sparse Core Ops, SparseCore 0:
  13.2 274.7 all-reduce.2
Sparse Core Ops, SparseCore 1:
  16.6 90.6 all-gather.1
  340.0 17.3 reduce-scatter.3
